TPU v7x, 256 devices: a whole 4x4x8 slice. The times are simulated.
256 devices in a mesh: segment: 4 (over y), ctx: 32 (over x_hi, z, core), tp: 2 (over x_lo).
Axes of the slice: x: 4 (x_hi: 2, x_lo: 2; x = x_hi * 2 + x_lo), y: 4, z: 8, core: 2. Of those that a mesh axis runs over, the one named last changes fastest.
Arguments:
- held: bfloat16 [4, 8192, 3584], P('segment', 'ctx'), may hold values from -6 to 6
- text: bfloat16 [8192, 3584], P('ctx'), may hold values from -6 to 6
- frames: bfloat16 [4096, 1024], P('ctx'), may hold values from -6 to 6
- join: int32 [64], P('ctx'), may hold values from 0 to 8128, as said below
- ln_gain: float32 [1024], replicated, may hold values from 0.1 to 1.9
- w_proj: bfloat16 [1024, 3584], P('tp'), may hold values from -0.1875 to 0.1875
- b_proj: float32 [3584], replicated, may hold values from -3 to 3
- norm_gain: float32 [3, 3584], replicated, may hold values from 0.1 to 1.9
- w_qkv: bfloat16 [3, 3584, 2304], P(None, 'ctx', 'tp'), may hold values from -0.09375 to 0.09375
- b_qkv: float32 [3, 2304], P(None, 'tp'), may hold values from -4 to 4
- w_out: bfloat16 [3, 1792, 3584], P(None, 'tp', 'ctx'), may hold values from -1.5 to 1.5
Outputs:
- segment_out: bfloat16 [4, 8192, 3584], P('segment', 'ctx')
Inputs may be any that keep to these rules, and one draw needn't show every extreme that they name: `join`: frames never intersect; the 2 frames f with f // 2 == d lie in order inside positions d * 256 to (d + 1) * 256 - 1.
All inputs are finite; a program needn't handle non-finite values.
Results may differ from a plain program's by a relative error of at most 0.015.
Values may be sent and summed in bfloat16 or wider, within the bound.
No kernel may reach another device: no remote copies, remote signals or barrier semaphores. Data moves between devices by JAX's collectives and lax.ppermute only.
A program may use at most 128 MiB of HBM per device.

v0:
```python
from functools import partial
import jax
import jax.numpy as jnp
from jax import lax
from jax.sharding import PartitionSpec as P

HD = 128
GROUP = 7
FRAME = 64


def shifted(value, axis, by):
    devices = lax.axis_size(axis)
    pairs = [(i, i + by) for i in range(devices) if 0 <= i + by < devices]
    return lax.ppermute(value, axis, pairs)


def update_state(softmax_state, query_flat, query_pos, keys_in, values_in, offset):
    peak_old, total_old, accum_old = softmax_state
    key_pos = jnp.arange(keys_in.shape[0], dtype=jnp.int32)
    scores = jnp.dot(query_flat, keys_in.T, preferred_element_type=jnp.float32) * HD ** (-0.5)
    allowed = key_pos[None, :] <= query_pos[:, None]
    scores = jnp.where(allowed, scores, -1e30)
    peak_new = jnp.maximum(peak_old, jnp.max(scores, axis=1))
    weights = jnp.where(allowed, jnp.exp(scores - peak_new[:, None]), 0.0)
    total_new = jnp.sum(weights, axis=1)
    accum_new = jnp.dot(weights.astype(jnp.bfloat16), values_in, preferred_element_type=jnp.float32)
    return (peak_new, total_new, accum_new)


def keep_state(softmax_state):
    return softmax_state


def on_device(held, text, frames, join, ln_gain, w_proj, b_proj, norm_gain, w_qkv, b_qkv, w_out):
    segment_id = lax.axis_index("segment")
    ctx_id = lax.axis_index("ctx")
    tp_id = lax.axis_index("tp")
    hidden_in = shifted(held[0], "segment", 1)
    tok_rows = hidden_in.shape[0]
    half_rows = tok_rows // 2
    layer_id = jnp.maximum(segment_id - 1, 0)
    weight_qkv = lax.dynamic_index_in_dim(w_qkv, layer_id, 0, keepdims=False)
    bias_qkv = lax.dynamic_index_in_dim(b_qkv, layer_id, 0, keepdims=False)
    layer_gain = lax.dynamic_index_in_dim(norm_gain, layer_id, 0, keepdims=False)
    weight_out = lax.dynamic_index_in_dim(w_out, layer_id, 0, keepdims=False)
    inputs = hidden_in.astype(jnp.float32)
    normed = (
        inputs * lax.rsqrt(jnp.mean(inputs * inputs, axis=1, keepdims=True) + 1e-06) * layer_gain
    ).astype(jnp.bfloat16)
    merged = jnp.dot(
        normed,
        lax.all_gather(weight_qkv, "ctx", axis=0, tiled=True),
        preferred_element_type=jnp.float32,
    )
    merged = (merged + bias_qkv).astype(jnp.bfloat16)
    query_cols = GROUP * HD
    queries = merged[:, :query_cols]
    key_part = merged[:, query_cols : query_cols + HD]
    value_part = merged[:, query_cols + HD : query_cols + 2 * HD]
    local_steps = jnp.arange(half_rows, dtype=jnp.int32)
    first_pos = ctx_id * tok_rows + local_steps
    second_q = queries[half_rows:]
    second_pos = ctx_id * tok_rows + half_rows + local_steps
    first_flat = queries[:half_rows].reshape(half_rows * GROUP, HD)
    second_flat = second_q.reshape(half_rows * GROUP, HD)
    first_qpos = jnp.repeat(first_pos, GROUP)
    second_qpos = jnp.repeat(second_pos, GROUP)
    flat_rows = half_rows * GROUP
    empty = (
        jnp.full((flat_rows,), -1e30, jnp.float32),
        jnp.zeros((flat_rows,), jnp.float32),
        jnp.zeros((flat_rows, HD), jnp.float32),
    )
    carried = (empty, empty)
    offset = jnp.int32(0)
    keys_in = lax.all_gather(key_part, "ctx", axis=0, tiled=True)
    values_in = lax.all_gather(value_part, "ctx", axis=0, tiled=True)
    updated = []
    for softmax_state, query_flat, query_pos in (
        (carried[0], first_flat, first_qpos),
        (carried[1], second_flat, second_qpos),
    ):
        step_fn = partial(
            update_state,
            query_flat=query_flat,
            query_pos=query_pos,
            keys_in=keys_in,
            values_in=values_in,
            offset=offset,
        )
        updated.append(lax.cond(offset <= jnp.max(query_pos), step_fn, keep_state, softmax_state))

    def finish(softmax_state):
        return (
            (softmax_state[2] / softmax_state[1][:, None])
            .astype(jnp.bfloat16)
            .reshape(half_rows, GROUP * HD)
        )

    first_out = finish(updated[0])
    second_out = finish(updated[1])
    attended = jnp.concatenate([first_out, second_out], axis=0)
    partial_model = jnp.dot(
        attended,
        lax.all_gather(weight_out, "ctx", axis=1, tiled=True),
        preferred_element_type=jnp.float32,
    )
    positions = ctx_id * tok_rows + jnp.arange(tok_rows, dtype=jnp.int32)[:, None]
    starts = join[None, :]
    inside = (positions >= starts) & (positions < starts + FRAME)
    frame_base = (jnp.arange(join.shape[0], dtype=jnp.int32) * FRAME)[None, :]
    source = jnp.sum(jnp.where(inside, frame_base + positions - starts, 0), axis=1)
    is_vision = jnp.any(inside, axis=1)

    def vision_term():
        frame_in = frames.astype(jnp.float32)
        center = jnp.mean(frame_in, axis=1, keepdims=True)
        spread = jnp.mean((frame_in - center) * (frame_in - center), axis=1, keepdims=True)
        normed_frames = ((frame_in - center) * lax.rsqrt(spread + 1e-06) * ln_gain).astype(
            jnp.bfloat16
        )
        vis_width = w_proj.shape[0]
        normed_half = lax.dynamic_slice_in_dim(normed_frames, tp_id * vis_width, vis_width, 1)
        projected = jnp.dot(normed_half, w_proj, preferred_element_type=jnp.float32)
        return jnp.where(is_vision[:, None], jnp.take(projected, source, axis=0), 0.0)

    def model_term():
        return partial_model

    is_first = segment_id == 0
    section_term = lax.cond(is_first, vision_term, model_term)
    baseline = jnp.where(
        is_first, jnp.where(is_vision[:, None], b_proj[None, :], text.astype(jnp.float32)), inputs
    )
    summed = lax.psum(section_term.astype(jnp.bfloat16), "tp").astype(jnp.float32)
    result = (baseline + summed).astype(jnp.bfloat16)
    return result[None]


def solution(mesh):
    return jax.shard_map(
        on_device,
        mesh=mesh,
        in_specs=(
            P("segment", "ctx", None),
            P("ctx", None),
            P("ctx", None),
            P("ctx"),
            P(),
            P("tp", None),
            P(),
            P(),
            P(None, "ctx", "tp"),
            P(None, "tp"),
            P(None, "tp", "ctx"),
        ),
        out_specs=P("segment", "ctx", None),
        check_vma=False,
    )
```

profile of v0, /device:TPU:1, one launch (start us, length us, event | category | flops | bytes accessed | tf_op | source)
XLA Modules:
  0.0 459.2 jit_solution(11434149428011326203)
XLA Ops:
  6.5 1.1 copy-done
  7.7 0.7 constant_dynamic-slice_fusion.1
  8.5 4.1 collective-permute-start
  12.6 0.7 dynamic-slice_reduce_fusion.1
  13.4 0.9 dynamic-slice_reduce_fusion
  14.2 37.2 %collective-permute-done = bf16[256,3584]{1,0:T(8,128)(2,1)S(1)} collective-permute-done((bf16[256,3584]{1,0:T(8,128)(2,1)}, bf16[256,3584]{1,0:T(8,128)(2,1)S(1)}, u32[]{:S(2)}, u32[]{:S(2)}) %collective-permute-start) | collective-permute-done | bytes 1835040 | tf_op jit(solution)/shard_map/ppermute | solution.py:15
  51.5 0.4 fusion.31
  51.9 63.3 %all-gather.11.cloned.1.call-done = bf16[1,3584,1152]{2,1,0:T(8,128)(2,1)} async-done(((bf16[1,112,1152]{2,1,0:T(8,128)(2,1)}), bf16[1,3584,1152]{2,1,0:T(8,128)(2,1)}) %all-gather.11.cloned.1.call-update) | async-done | bytes 8257552 | tf_op jit(solution)/shard_map/all_gather | solution.py:53
  115.3 5.9 %fusion.37 = bf16[256,1152]{1,0:T(8,128)(2,1)S(1)} fusion(bf16[1,3584,1152]{2,1,0:T(8,128)(2,1)} %all-gather.11.cloned.1.call-done, bf16[256,3584]{1,0:T(8,128)(2,1)S(1)} %collective-permute-done, f32[3584]{0:T(1024)S(1)} %dynamic-slice_reduce_fusion, f32[256]{0:T(256)S(1)} %add_rsqrt_fusion.1, f32[1152]{0:T(1024)S(1)} %dynamic-slice_reduce_fusion.1), kind=kOutput, calls=%fused_computation.56 | convolution fusion | flops 2118189056 | bytes 10702336 | tf_op jit(solution)/shard_map/dot_general | solution.py:51
  121.2 0.6 fusion.49
  121.9 0.7 all-gather.9.cloned.1.call-update
  122.7 1.6 constant_dynamic-slice_fusion
  124.4 0.7 broadcast_reduce_fusion.1
  125.7 0.7 broadcast_reduce_fusion
  127.2 71.2 %all-gather.7.cloned.1.call-done = bf16[8192,128]{1,0:T(8,128)(2,1)} async-done(((bf16[256,128]{1,0:T(8,128)(2,1)}), bf16[8192,128]{1,0:T(8,128)(2,1)}) %all-gather.7.cloned.1.call-update) | async-done | bytes 2097168 | tf_op jit(solution)/shard_map/all_gather | solution.py:77
  198.4 79.4 %all-gather.9.cloned.1.call-done = bf16[8192,128]{1,0:T(8,128)(2,1)} async-done(((bf16[256,128]{1,0:T(8,128)(2,1)}), bf16[8192,128]{1,0:T(8,128)(2,1)}) %all-gather.9.cloned.1.call-update) | async-done | bytes 2097168 | tf_op jit(solution)/shard_map/all_gather | solution.py:78
  277.8 42.2 %conditional.3 = (f32[896]{0:T(1024)S(1)}, f32[896,128]{1,0:T(8,128)S(1)}) conditional(s32[]{:T(128)} %convert_element_type.51, () %tuple.27, (s32[128,7]{1,0:T(8,128)S(1)}, bf16[256,1152]{1,0:T(8,128)(2,1)S(1)}, bf16[8192,128]{1,0:T(8,128)(2,1)}, bf16[8192,128]{1,0:T(8,128)(2,1)}) %tuple.28), branch_computations={%region_3.4_spmd, %region_4.7_spmd} | conditional | flops 3875535872 | bytes 102308392 | solution.py:92
  278.3 14.2 %fusion = (f32[896]{0:T(1024)S(1)}, f32[896,8192]{1,0:T(8,128)}) fusion(s32[896]{0:T(1024)S(1)} %le.30, bf16[896,128]{1,0:T(8,128)(2,1)S(1)} %reshape.63, bf16[8192,128]{1,0:T(8,128)(2,1)} %get-tuple-element.43), kind=kOutput, calls=%fused_computation.4 | convolution fusion | flops 1908407424 | bytes 31693824 | tf_op jit(solution)/shard_map/cond/branch_1_fun/dot_general | solution.py:21
  292.5 13.1 %fusion.3 = f32[896,128]{1,0:T(8,128)S(1)} fusion(bf16[8192,128]{1,0:T(8,128)(2,1)S(1)} %copy-done.7, f32[896,8192]{1,0:T(8,128)} %get-tuple-element.86, f32[896]{0:T(1024)S(1)} %broadcast_maximum_fusion, s32[896]{0:T(1024)S(1)} %le.30), kind=kOutput, calls=%fused_computation.7 | convolution fusion | flops 1923088384 | bytes 31923200 | tf_op jit(solution)/shard_map/cond/branch_1_fun/dot_general | solution.py:27
  305.6 14.4 %fusion.2 = f32[896]{0:T(1024)S(1)} fusion(f32[896,8192]{1,0:T(8,128)} %get-tuple-element.86, f32[896]{0:T(1024)S(1)} %broadcast_maximum_fusion, s32[896]{0:T(1024)S(1)} %le.30), kind=kLoop, calls=%fused_computation.6 | loop fusion | flops 44039296 | bytes 29370880 | tf_op jit(solution)/shard_map/cond/branch_1_fun/reduce_sum | solution.py:26
  320.6 42.8 %conditional.4 = (f32[896]{0:T(1024)S(1)}, f32[896,128]{1,0:T(8,128)S(1)}) conditional(s32[]{:T(128)} %convert_element_type.55, () %tuple.29, (s32[128,7]{1,0:T(8,128)S(1)}, bf16[256,1152]{1,0:T(8,128)(2,1)S(1)}, bf16[8192,128]{1,0:T(8,128)(2,1)}, bf16[8192,128]{1,0:T(8,128)(2,1)}) %tuple.30), branch_computations={%region_8.9_spmd, %region_9.12_spmd} | conditional | flops 3875535872 | bytes 102308392 | solution.py:92
  321.3 14.4 %fusion.8 = (f32[896]{0:T(1024)S(1)}, f32[896,8192]{1,0:T(8,128)}) fusion(s32[896]{0:T(1024)S(1)} %le.38, bf16[896,128]{1,0:T(8,128)(2,1)S(1)} %reshape.64, bf16[8192,128]{1,0:T(8,128)(2,1)} %get-tuple-element.47), kind=kOutput, calls=%fused_computation.15 | convolution fusion | flops 1908407424 | bytes 31693824 | tf_op jit(solution)/shard_map/cond/branch_1_fun/dot_general | solution.py:21
  335.7 13.0 %fusion.11 = f32[896,128]{1,0:T(8,128)S(1)} fusion(bf16[8192,128]{1,0:T(8,128)(2,1)S(1)} %copy-done.8, f32[896,8192]{1,0:T(8,128)} %get-tuple-element.88, f32[896]{0:T(1024)S(1)} %broadcast_maximum_fusion.1, s32[896]{0:T(1024)S(1)} %le.38), kind=kOutput, calls=%fused_computation.18 | convolution fusion | flops 1923088384 | bytes 31923200 | tf_op jit(solution)/shard_map/cond/branch_1_fun/dot_general | solution.py:27
  348.8 14.6 %fusion.10 = f32[896]{0:T(1024)S(1)} fusion(f32[896,8192]{1,0:T(8,128)} %get-tuple-element.88, f32[896]{0:T(1024)S(1)} %broadcast_maximum_fusion.1, s32[896]{0:T(1024)S(1)} %le.38), kind=kLoop, calls=%fused_computation.17 | loop fusion | flops 44039296 | bytes 29370880 | tf_op jit(solution)/shard_map/cond/branch_1_fun/reduce_sum | solution.py:26
  363.8 7.7 %all-gather.13.cloned.1.call-done = bf16[1,896,3584]{1,2,0:T(8,128)(2,1)} async-done(((bf16[1,896,112]{1,2,0:T(8,128)(2,1)}), bf16[1,896,3584]{1,2,0:T(8,128)(2,1)}) %all-gather.13.cloned.1.call-update) | async-done | bytes 6422544 | tf_op jit(solution)/shard_map/all_gather | solution.py:106
  371.6 6.2 %fusion.27 = bf16[256,3584]{1,0:T(8,128)(2,1)} fusion(bf16[1,896,3584]{1,2,0:T(8,128)(2,1)} %all-gather.13.cloned.1.call-done, bf16[128,896]{1,0:T(8,128)(2,1)S(1)} %reshape.68, bf16[128,896]{1,0:T(8,128)(2,1)S(1)} %reshape.67), kind=kOutput, calls=%fused_computation.45 | convolution fusion | flops 1645084672 | bytes 8716288 | tf_op jit(solution)/shard_map/dot_general | solution.py:104
  377.7 7.3 %conditional.5 = (bf16[256,3584]{1,0:T(8,128)(2,1)}) conditional(s32[]{:T(128)} %convert_element_type.50, bf16[256,3584]{1,0:T(8,128)(2,1)} %fusion.27, (pred[256]{0:T(512)(128)(4,1)S(1)}, pred[256,2]{0,1:T(4,128)(4,1)S(1)}, bf16[128,1024]{1,0:T(8,128)(2,1)S(1)}, f32[1024]{0:T(1024)S(1)}, s32[]{:T(128)}, /*index=5*/bf16[512,3584]{1,0:T(8,128)(2,1)}, ...), branch_computations={%region_13.14_spmd, %region_14.17_spmd} | conditional | flops 472585344 | bytes 13264226 | solution.py:132
  378.2 2.7 fusion.18
  381.0 1.7 gather_fusion
  382.8 2.2 select_select_fusion
  385.0 62.8 %all-reduce.2.cloned.1.call-done = bf16[256,3584]{1,0:T(8,128)(2,1)} async-done(((bf16[256,3584]{1,0:T(8,128)(2,1)}), bf16[256,3584]{1,0:T(8,128)(2,1)}) %all-reduce.2.cloned.1.call-update) | async-done | bytes 1835024 | tf_op jit(solution)/shard_map/psum | solution.py:136
  447.9 4.8 %fusion.41 = bf16[1,256,3584]{2,1,0:T(8,128)(2,1)} fusion(bf16[256,3584]{1,0:T(8,128)(2,1)} %all-reduce.2.cloned.1.call-done, bf16[256,3584]{1,0:T(8,128)(2,1)} %copy-done.2, bf16[256,3584]{1,0:T(8,128)(2,1)} %param.18, f32[3584]{0:T(1024)S(1)} %copy-done.4, pred[256]{0:T(512)(128)(4,1)S(1)} %get-tuple-element.83, pred[]{:T(512)S(6)} %eq.3), kind=kLoop, calls=%fused_computation.57 | loop fusion | flops 6422528 | bytes 7354625 | tf_op jit(solution)/shard_map/broadcast_in_dim | solution.py:138
  (59 shorter events, 2.9 us)
Async XLA Ops:
  6.5 1.1 copy-start
  6.5 108.7 %all-gather.11.cloned.1.call-start = ((), (), s32[]{:S(2)}) async-start(), calls=%async_computation.3 | async-start | bytes 8515584 | tf_op jit(solution)/shard_map/all_gather | solution.py:53
  8.4 190.0 %all-gather.7.cloned.1.call-start = ((), (), s32[]{:S(2)}) async-start(), calls=%async_computation | async-start | bytes 2162688 | tf_op jit(solution)/shard_map/all_gather | solution.py:77
  8.5 43.0 %collective-permute-start = (bf16[256,3584]{1,0:T(8,128)(2,1)}, bf16[256,3584]{1,0:T(8,128)(2,1)S(1)}, u32[]{:S(2)}, u32[]{:S(2)}) collective-permute-start(bf16[256,3584]{1,0:T(8,128)(2,1)} %bitcast.20), channel_id=1, source_target_pairs={{0,64},{64,128},{128,192},{1,65},{65,129},{129,193},{2,66},{66,130... | collective-permute-start | bytes 5505032 | tf_op jit(solution)/shard_map/ppermute | solution.py:15
  51.5 69.7 %copy-start.2 = (bf16[256,3584]{1,0:T(8,128)(2,1)}, bf16[256,3584]{1,0:T(8,128)(2,1)S(1)}, u32[]{:S(2)}) copy-start(bf16[256,3584]{1,0:T(8,128)(2,1)S(1)} %collective-permute-done) | copy-start | bytes 5505028
  51.9 75.1 %copy-start.5 = (s32[2]{0:T(128)S(1)}, s32[2]{0:T(128)}, u32[]{:S(2)}) copy-start(s32[2]{0:T(128)} %param.20) | copy-start | bytes 28
  121.9 155.9 %all-gather.9.cloned.1.call-start = ((), (), s32[]{:S(2)}) async-start(), calls=%async_computation.1 | async-start | bytes 2162688 | tf_op jit(solution)/shard_map/all_gather | solution.py:78
  122.6 248.9 %all-gather.13.cloned.1.call-start = ((), (), s32[]{:S(2)}) async-start(), calls=%async_computation.4 | async-start | bytes 6623232 | tf_op jit(solution)/shard_map/all_gather | solution.py:106
  124.3 323.5 %all-reduce.2.cloned.1.call-start = ((), (), s32[]{:S(2)}) async-start(), calls=%async_computation.2 | async-start | bytes 3670016 | tf_op jit(solution)/shard_map/psum | solution.py:136
  278.3 14.2 %copy-start.7 = (bf16[8192,128]{1,0:T(8,128)(2,1)S(1)}, bf16[8192,128]{1,0:T(8,128)(2,1)}, u32[]{:S(2)}) copy-start(bf16[8192,128]{1,0:T(8,128)(2,1)} %get-tuple-element.44) | copy-start | bytes 6291460 | tf_op jit(solution)/shard_map/cond
  320.6 51.0 %copy-start.3 = (bf16[128,1024]{1,0:T(8,128)(2,1)S(1)}, bf16[128,1024]{1,0:T(8,128)(2,1)}, u32[]{:S(2)}) copy-start(bf16[128,1024]{1,0:T(8,128)(2,1)} %param.19) | copy-start | bytes 786436
  320.6 51.0 %copy-start.6 = (f32[1024]{0:T(1024)S(1)}, f32[1024]{0:T(1024)}, u32[]{:S(2)}) copy-start(f32[1024]{0:T(1024)} %param.21) | copy-start | bytes 12292
  321.3 14.4 %copy-start.8 = (bf16[8192,128]{1,0:T(8,128)(2,1)S(1)}, bf16[8192,128]{1,0:T(8,128)(2,1)}, u32[]{:S(2)}) copy-start(bf16[8192,128]{1,0:T(8,128)(2,1)} %get-tuple-element.48) | copy-start | bytes 6291460 | tf_op jit(solution)/shard_map/cond
  377.7 70.1 %copy-start.4 = (f32[3584]{0:T(1024)S(1)}, f32[3584]{0:T(1024)}, u32[]{:S(2)}) copy-start(f32[3584]{0:T(1024)} %param.23) | copy-start | bytes 43012
  385.0 67.6 %copy-start.1 = (bf16[3,112,1152]{2,1,0:T(8,128)(2,1)S(1)}, bf16[3,112,1152]{2,1,0:T(8,128)(2,1)}, u32[]{:S(2)}) copy-start(bf16[3,112,1152]{2,1,0:T(8,128)(2,1)} %param.25) | copy-start | bytes 2322436
Sparse Core Ops, SparseCore 0:
  10.0 105.1 all-gather.10
  122.0 76.3 all-gather.6
  201.2 76.5 all-gather.8
  280.3 91.2 all-gather.12
  385.2 62.6 all-reduce.1
where the time goes:
time: 460 us; the launch traced here: 459 us
  waiting for transfers between devices  322 us (70%)
  matrix products  69.6 us (15%)
  other arithmetic  38.9 us (8%)
  between operations  14.4 us (3%)
  local copies, waits for them, and re-layouts  9.21 us (2%)
    all_gather x1, waiting for transfers between devices, on_device(): values_in = lax.all_gather(value_part, 'ctx', axis=0, tiled=True)  79.4 us
    all_gather x1, waiting for transfers between devices, on_device(): keys_in = lax.all_gather(key_part, 'ctx', axis=0, tiled=True)  71.2 us
    all_gather x1, waiting for transfers between devices, on_device(): lax.all_gather(weight_qkv, 'ctx', axis=0, tiled=True)  63.3 us
    psum x1, waiting for transfers between devices, on_device(): lax.psum(section_term.astype(jnp.bfloat16), 'tp').astype(jnp.float32)  62.8 us
    ppermute x1, waiting for transfers between devices, shifted(): return lax.ppermute(value, axis, pairs)  37.2 us
    reduce_sum x2, other arithmetic, update_state(): total_new = jnp.sum(weights, axis=1)  29.1 us
    dot_general x2, matrix products, update_state(): jnp.dot(query_flat, keys_in.T, preferred_element_type=jnp.float32)  28.6 us
    dot_general x2, matrix products, update_state(): jnp.dot(weights.astype(jnp.bfloat16), values_in, preferred_element_type=j...  26.1 us
  transfers between devices with their start and end apart: 6, of which 6 were waited for; matrix products, arithmetic and copies ran while one was open for 20% of the time, Pallas kernels for 0%

commit v1 on v0

--- a/solution.py
+++ b/solution.py
@@ -74,7 +74,9 @@
     )
     carried = (empty, empty)
     offset = jnp.int32(0)
-    keys_in = lax.all_gather(key_part, "ctx", axis=0, tiled=True)
+    keys_in = jnp.concatenate(
+        lax.all_to_all(jnp.stack([key_part] * lax.axis_size("ctx")), "ctx", 0, 0), axis=0
+    )
     values_in = lax.all_gather(value_part, "ctx", axis=0, tiled=True)
     updated = []
     for softmax_state, query_flat, query_pos in (

time: 460 us -> 393 us (0.85)
  waiting for transfers between devices: 322 us -> 248 us
    all_gather x1 -> x0, waiting for transfers between devices: 71.2 us -> none  [on_device(): keys_in = lax.all_gather(key_part, 'ctx', axis=0, tiled=True)]
    all_gather x1, waiting for transfers between devices: 79.4 us -> 23.5 us  [on_device(): values_in = lax.all_gather(value_part, 'ctx', axis=0, tiled=True)]
    all_to_all x0 -> x1, waiting for transfers between devices: none -> 51.3 us  [on_device(): lax.all_to_all(jnp.stack([key_part] * lax.axis_size('ctx')), 'ctx', 0, 0)]
  transfers between devices with their start and end apart: 6 -> 6, of which waited for: 6 -> 6; matrix products, arithmetic and copies ran while one was open for 20% -> 23% of each run, Pallas kernels for 0% -> 0%
where the time goes in v1:
time: 393 us; the launch traced here: 392 us
  waiting for transfers between devices  248 us (63%)
  matrix products  67.6 us (17%)
  other arithmetic  39 us (10%)
  between operations  14.5 us (4%)
  local copies, waits for them, and re-layouts  13.8 us (4%)
  starting transfers between devices  8.64 us (2%)
    all_gather x1, waiting for transfers between devices, on_device(): lax.all_gather(weight_qkv, 'ctx', axis=0, tiled=True)  63.3 us
    psum x1, waiting for transfers between devices, on_device(): lax.psum(section_term.astype(jnp.bfloat16), 'tp').astype(jnp.float32)  62.9 us
    all_to_all x1, waiting for transfers between devices, on_device(): lax.all_to_all(jnp.stack([key_part] * lax.axis_size('ctx')), 'ctx', 0, 0)  51.3 us
    ppermute x1, waiting for transfers between devices, shifted(): return lax.ppermute(value, axis, pairs)  37.2 us
    reduce_sum x2, other arithmetic, update_state(): total_new = jnp.sum(weights, axis=1)  29.1 us
    dot_general x2, matrix products, update_state(): jnp.dot(weights.astype(jnp.bfloat16), values_in, preferred_element_type=j...  26.1 us
    dot_general x2, matrix products, update_state(): jnp.dot(query_flat, keys_in.T, preferred_element_type=jnp.float32)  25.8 us
    all_gather x1, waiting for transfers between devices, on_device(): values_in = lax.all_gather(value_part, 'ctx', axis=0, tiled=True)  23.5 us
  transfers between devices with their start and end apart: 6, of which 6 were waited for; matrix products, arithmetic and copies ran while one was open for 23% of the time, Pallas kernels for 0%

profile of v1, /device:TPU:1, one launch (start us, length us, event | category | flops | bytes accessed | tf_op | source)
XLA Modules:
  0.0 391.9 jit_solution(2587796702158688031)
XLA Ops:
  6.5 1.1 copy-done
  8.5 4.1 %collective-permute-start = (bf16[256,3584]{1,0:T(8,128)(2,1)}, bf16[256,3584]{1,0:T(8,128)(2,1)S(1)}, u32[]{:S(2)}, u32[]{:S(2)}) collective-permute-start(bf16[256,3584]{1,0:T(8,128)(2,1)} %bitcast.23), channel_id=1, source_target_pairs={{0,64},{64,128},{128,192},{1,65},{65,129},{129,193},{2,66},{66,130... | collective-permute-start | bytes 5505032 | tf_op jit(solution)/shard_map/ppermute | solution.py:15
  12.6 0.7 dynamic-slice_reduce_fusion.1
  13.4 0.9 dynamic-slice_reduce_fusion
  14.2 37.2 %collective-permute-done = bf16[256,3584]{1,0:T(8,128)(2,1)S(1)} collective-permute-done((bf16[256,3584]{1,0:T(8,128)(2,1)}, bf16[256,3584]{1,0:T(8,128)(2,1)S(1)}, u32[]{:S(2)}, u32[]{:S(2)}) %collective-permute-start) | collective-permute-done | bytes 1835040 | tf_op jit(solution)/shard_map/ppermute | solution.py:15
  51.9 63.3 %all-gather.8.cloned.1.call-done = bf16[1,3584,1152]{2,1,0:T(8,128)(2,1)} async-done(((bf16[1,112,1152]{2,1,0:T(8,128)(2,1)}), bf16[1,3584,1152]{2,1,0:T(8,128)(2,1)}) %all-gather.8.cloned.1.call-update) | async-done | bytes 8257552 | tf_op jit(solution)/shard_map/all_gather | solution.py:53
  115.3 6.8 %fusion.37 = bf16[256,1152]{1,0:T(8,128)(2,1)} fusion(bf16[1,3584,1152]{2,1,0:T(8,128)(2,1)} %all-gather.8.cloned.1.call-done, bf16[256,3584]{1,0:T(8,128)(2,1)S(1)} %collective-permute-done, f32[3584]{0:T(1024)S(1)} %dynamic-slice_reduce_fusion, f32[256]{0:T(256)S(1)} %add_rsqrt_fusion.1, f32[1152]{0:T(1024)S(1)} %dynamic-slice_reduce_fusion.1), kind=kOutput, calls=%fused_computation.56 | convolution fusion | flops 2118189056 | bytes 10702336 | tf_op jit(solution)/shard_map/dot_general | solution.py:51
  122.0 1.5 fusion.49
  123.6 1.6 constant_dynamic-slice_fusion
  125.3 1.8 stack.2
  127.1 4.4 %all-to-all-start = ((bf16[32,256,128]{2,1,0:T(8,128)(2,1)}), bf16[32,256,128]{2,1,0:T(8,128)(2,1)S(1)}, u32[]{:S(2)}, u32[]{:S(2)}) async-start(bf16[32,256,128]{2,1,0:T(8,128)(2,1)} %stack.2), calls=%async_computation | async-start | bytes 4194304 | tf_op jit(solution)/shard_map/all_to_all | solution.py:78
  131.5 0.8 broadcast_reduce_fusion.1
  134.5 51.3 %all-to-all-done = bf16[32,256,128]{2,1,0:T(8,128)(2,1)S(1)} async-done(((bf16[32,256,128]{2,1,0:T(8,128)(2,1)}), bf16[32,256,128]{2,1,0:T(8,128)(2,1)S(1)}, u32[]{:S(2)}, u32[]{:S(2)}) %all-to-all-start) | async-done | bytes 2097184 | tf_op jit(solution)/shard_map/all_to_all | solution.py:78
  185.8 23.5 %all-gather.6.cloned.1.call-done = bf16[8192,128]{1,0:T(8,128)(2,1)} async-done(((bf16[256,128]{1,0:T(8,128)(2,1)}), bf16[8192,128]{1,0:T(8,128)(2,1)}) %all-gather.6.cloned.1.call-update) | async-done | bytes 2097168 | tf_op jit(solution)/shard_map/all_gather | solution.py:80
  209.4 41.9 %conditional.3 = (f32[896]{0:T(1024)S(1)}, f32[896,128]{1,0:T(8,128)S(1)}) conditional(s32[]{:T(128)} %convert_element_type.51, () %tuple.27, (s32[128,7]{1,0:T(8,128)S(1)}, bf16[256,1152]{1,0:T(8,128)(2,1)}, bf16[8192,128]{1,0:T(8,128)(2,1)S(1)}, bf16[8192,128]{1,0:T(8,128)(2,1)}) %tuple.51), branch_computations={%region_3.4_spmd, %region_4.7_spmd} | conditional | flops 3875535872 | bytes 102308392 | solution.py:94
  209.6 1.0 slice.13
  210.8 12.8 %fusion = (f32[896]{0:T(1024)S(1)}, f32[896,8192]{1,0:T(8,128)}) fusion(s32[896]{0:T(1024)S(1)} %le.30, bf16[896,128]{1,0:T(8,128)(2,1)S(1)} %reshape.67, bf16[8192,128]{1,0:T(8,128)(2,1)S(1)} %get-tuple-element.43), kind=kOutput, calls=%fused_computation.4 | convolution fusion | flops 1908407424 | bytes 31693824 | tf_op jit(solution)/shard_map/cond/branch_1_fun/dot_general | solution.py:21
  223.6 13.1 %fusion.3 = f32[896,128]{1,0:T(8,128)S(1)} fusion(bf16[8192,128]{1,0:T(8,128)(2,1)S(1)} %copy-done.7, f32[896,8192]{1,0:T(8,128)} %get-tuple-element.86, f32[896]{0:T(1024)S(1)} %broadcast_maximum_fusion, s32[896]{0:T(1024)S(1)} %le.30), kind=kOutput, calls=%fused_computation.7 | convolution fusion | flops 1923088384 | bytes 31923200 | tf_op jit(solution)/shard_map/cond/branch_1_fun/dot_general | solution.py:27
  236.7 14.5 %fusion.2 = f32[896]{0:T(1024)S(1)} fusion(f32[896,8192]{1,0:T(8,128)} %get-tuple-element.86, f32[896]{0:T(1024)S(1)} %broadcast_maximum_fusion, s32[896]{0:T(1024)S(1)} %le.30), kind=kLoop, calls=%fused_computation.6 | loop fusion | flops 44039296 | bytes 29370880 | tf_op jit(solution)/shard_map/cond/branch_1_fun/reduce_sum | solution.py:26
  251.9 42.2 %conditional.4 = (f32[896]{0:T(1024)S(1)}, f32[896,128]{1,0:T(8,128)S(1)}) conditional(s32[]{:T(128)} %convert_element_type.55, () %tuple.29, (s32[128,7]{1,0:T(8,128)S(1)}, bf16[256,1152]{1,0:T(8,128)(2,1)}, bf16[8192,128]{1,0:T(8,128)(2,1)S(1)}, bf16[8192,128]{1,0:T(8,128)(2,1)}) %tuple.52), branch_computations={%region_8.9_spmd, %region_9.12_spmd} | conditional | flops 3875535872 | bytes 102308392 | solution.py:94
  252.1 1.0 slice.14
  253.3 13.0 %fusion.8 = (f32[896]{0:T(1024)S(1)}, f32[896,8192]{1,0:T(8,128)}) fusion(s32[896]{0:T(1024)S(1)} %le.38, bf16[896,128]{1,0:T(8,128)(2,1)S(1)} %reshape.68, bf16[8192,128]{1,0:T(8,128)(2,1)S(1)} %get-tuple-element.47), kind=kOutput, calls=%fused_computation.15 | convolution fusion | flops 1908407424 | bytes 31693824 | tf_op jit(solution)/shard_map/cond/branch_1_fun/dot_general | solution.py:21
  266.3 13.1 %fusion.11 = f32[896,128]{1,0:T(8,128)S(1)} fusion(bf16[8192,128]{1,0:T(8,128)(2,1)S(1)} %copy-done.8, f32[896,8192]{1,0:T(8,128)} %get-tuple-element.88, f32[896]{0:T(1024)S(1)} %broadcast_maximum_fusion.1, s32[896]{0:T(1024)S(1)} %le.38), kind=kOutput, calls=%fused_computation.18 | convolution fusion | flops 1923088384 | bytes 31923200 | tf_op jit(solution)/shard_map/cond/branch_1_fun/dot_general | solution.py:27
  279.4 14.6 %fusion.10 = f32[896]{0:T(1024)S(1)} fusion(f32[896,8192]{1,0:T(8,128)} %get-tuple-element.88, f32[896]{0:T(1024)S(1)} %broadcast_maximum_fusion.1, s32[896]{0:T(1024)S(1)} %le.38), kind=kLoop, calls=%fused_computation.17 | loop fusion | flops 44039296 | bytes 29370880 | tf_op jit(solution)/shard_map/cond/branch_1_fun/reduce_sum | solution.py:26
  294.5 9.8 %all-gather.10.cloned.1.call-done = bf16[1,896,3584]{1,2,0:T(8,128)(2,1)} async-done(((bf16[1,896,112]{1,2,0:T(8,128)(2,1)}), bf16[1,896,3584]{1,2,0:T(8,128)(2,1)}) %all-gather.10.cloned.1.call-update) | async-done | bytes 6422544 | tf_op jit(solution)/shard_map/all_gather | solution.py:108
  304.3 6.2 %fusion.27 = bf16[256,3584]{1,0:T(8,128)(2,1)} fusion(bf16[1,896,3584]{1,2,0:T(8,128)(2,1)} %all-gather.10.cloned.1.call-done, bf16[128,896]{1,0:T(8,128)(2,1)S(1)} %reshape.74, bf16[128,896]{1,0:T(8,128)(2,1)S(1)} %reshape.73), kind=kOutput, calls=%fused_computation.45 | convolution fusion | flops 1645084672 | bytes 8716288 | tf_op jit(solution)/shard_map/dot_general | solution.py:106
  310.4 7.3 %conditional.5 = (bf16[256,3584]{1,0:T(8,128)(2,1)}) conditional(s32[]{:T(128)} %convert_element_type.50, bf16[256,3584]{1,0:T(8,128)(2,1)} %fusion.27, (pred[256]{0:T(512)(128)(4,1)S(1)}, pred[256,2]{0,1:T(4,128)(4,1)S(1)}, bf16[128,1024]{1,0:T(8,128)(2,1)S(1)}, f32[1024]{0:T(1024)S(1)}, s32[]{:T(128)}, /*index=5*/bf16[512,3584]{1,0:T(8,128)(2,1)}, ...), branch_computations={%region_13.14_spmd, %region_14.17_spmd} | conditional | flops 472585344 | bytes 13264226 | solution.py:134
  310.9 2.7 fusion.18
  313.7 1.7 gather_fusion
  315.5 2.2 select_select_fusion
  317.7 62.9 %all-reduce.2.cloned.1.call-done = bf16[256,3584]{1,0:T(8,128)(2,1)} async-done(((bf16[256,3584]{1,0:T(8,128)(2,1)}), bf16[256,3584]{1,0:T(8,128)(2,1)}) %all-reduce.2.cloned.1.call-update) | async-done | bytes 1835024 | tf_op jit(solution)/shard_map/psum | solution.py:138
  380.6 4.8 %fusion.41 = bf16[1,256,3584]{2,1,0:T(8,128)(2,1)} fusion(bf16[256,3584]{1,0:T(8,128)(2,1)} %all-reduce.2.cloned.1.call-done, bf16[256,3584]{1,0:T(8,128)(2,1)} %copy-done.2, bf16[256,3584]{1,0:T(8,128)(2,1)} %param.18, f32[3584]{0:T(1024)S(1)} %copy-done.4, pred[256]{0:T(512)(128)(4,1)S(1)} %get-tuple-element.83, pred[]{:T(512)S(6)} %eq.3), kind=kLoop, calls=%fused_computation.57 | loop fusion | flops 6422528 | bytes 7354625 | tf_op jit(solution)/shard_map/broadcast_in_dim | solution.py:140
  (59 shorter events, 4.8 us)
Async XLA Ops:
  6.5 1.1 copy-start
  6.5 108.7 %all-gather.8.cloned.1.call-start = ((), (), s32[]{:S(2)}) async-start(), calls=%async_computation.3 | async-start | bytes 8515584 | tf_op jit(solution)/shard_map/all_gather | solution.py:53
  8.4 200.9 %all-gather.6.cloned.1.call-start = ((), (), s32[]{:S(2)}) async-start(), calls=%async_computation.1 | async-start | bytes 2162688 | tf_op jit(solution)/shard_map/all_gather | solution.py:80
  8.5 43.0 %collective-permute-start = (bf16[256,3584]{1,0:T(8,128)(2,1)}, bf16[256,3584]{1,0:T(8,128)(2,1)S(1)}, u32[]{:S(2)}, u32[]{:S(2)}) collective-permute-start(bf16[256,3584]{1,0:T(8,128)(2,1)} %bitcast.23), channel_id=1, source_target_pairs={{0,64},{64,128},{128,192},{1,65},{65,129},{129,193},{2,66},{66,130... | collective-permute-start | bytes 5505032 | tf_op jit(solution)/shard_map/ppermute | solution.py:15
  51.5 70.6 %copy-start.2 = (bf16[256,3584]{1,0:T(8,128)(2,1)}, bf16[256,3584]{1,0:T(8,128)(2,1)S(1)}, u32[]{:S(2)}) copy-start(bf16[256,3584]{1,0:T(8,128)(2,1)S(1)} %collective-permute-done) | copy-start | bytes 5505028
  51.9 82.4 %copy-start.5 = (s32[2]{0:T(128)S(1)}, s32[2]{0:T(128)}, u32[]{:S(2)}) copy-start(s32[2]{0:T(128)} %param.20) | copy-start | bytes 28
  123.6 180.7 %all-gather.10.cloned.1.call-start = ((), (), s32[]{:S(2)}) async-start(), calls=%async_computation.4 | async-start | bytes 6623232 | tf_op jit(solution)/shard_map/all_gather | solution.py:108
  127.1 58.8 %all-to-all-start = ((bf16[32,256,128]{2,1,0:T(8,128)(2,1)}), bf16[32,256,128]{2,1,0:T(8,128)(2,1)S(1)}, u32[]{:S(2)}, u32[]{:S(2)}) async-start(bf16[32,256,128]{2,1,0:T(8,128)(2,1)} %stack.2), calls=%async_computation | async-start | bytes 4194304 | tf_op jit(solution)/shard_map/all_to_all | solution.py:78
  131.4 249.2 %all-reduce.2.cloned.1.call-start = ((), (), s32[]{:S(2)}) async-start(), calls=%async_computation.2 | async-start | bytes 3670016 | tf_op jit(solution)/shard_map/psum | solution.py:138
  210.8 12.8 %copy-start.7 = (bf16[8192,128]{1,0:T(8,128)(2,1)S(1)}, bf16[8192,128]{1,0:T(8,128)(2,1)}, u32[]{:S(2)}) copy-start(bf16[8192,128]{1,0:T(8,128)(2,1)} %get-tuple-element.44) | copy-start | bytes 6291460 | tf_op jit(solution)/shard_map/cond
  251.9 52.4 %copy-start.3 = (bf16[128,1024]{1,0:T(8,128)(2,1)S(1)}, bf16[128,1024]{1,0:T(8,128)(2,1)}, u32[]{:S(2)}) copy-start(bf16[128,1024]{1,0:T(8,128)(2,1)} %param.19) | copy-start | bytes 786436
  251.9 52.4 %copy-start.6 = (f32[1024]{0:T(1024)S(1)}, f32[1024]{0:T(1024)}, u32[]{:S(2)}) copy-start(f32[1024]{0:T(1024)} %param.21) | copy-start | bytes 12292
  253.3 13.0 %copy-start.8 = (bf16[8192,128]{1,0:T(8,128)(2,1)S(1)}, bf16[8192,128]{1,0:T(8,128)(2,1)}, u32[]{:S(2)}) copy-start(bf16[8192,128]{1,0:T(8,128)(2,1)} %get-tuple-element.48) | copy-start | bytes 6291460 | tf_op jit(solution)/shard_map/cond
  310.4 70.2 %copy-start.4 = (f32[3584]{0:T(1024)S(1)}, f32[3584]{0:T(1024)}, u32[]{:S(2)}) copy-start(f32[3584]{0:T(1024)} %param.23) | copy-start | bytes 43012
  317.7 67.7 %copy-start.1 = (bf16[3,112,1152]{2,1,0:T(8,128)(2,1)S(1)}, bf16[3,112,1152]{2,1,0:T(8,128)(2,1)}, u32[]{:S(2)}) copy-start(bf16[3,112,1152]{2,1,0:T(8,128)(2,1)} %param.25) | copy-start | bytes 2322436
Sparse Core Ops, SparseCore 0:
  10.0 105.1 all-gather.7
  123.7 85.5 all-gather.5
  212.0 92.2 all-gather.9
  317.9 62.7 all-reduce.1
